TPU v7x, 256 devices: a whole 4x4x8 slice. The times are simulated.
256 devices in a mesh: row: 8 (over y, core), col: 32 (over z, x).
Axes of the slice: x: 4, y: 4, z: 8, core: 2. Of those that a mesh axis runs over, the one named last changes fastest.
Arguments:
- blocks: float32 [128, 32, 256, 256], P('row', 'col'), may hold values from -6 to 6
- panel_rows: int32 [2, 64], P(None, 'row'), may hold values from -1 to 767, as said below
- target_slots: int32 [2, 128, 32], P(None, 'row', 'col'), may hold values from -1 to 7, as said below
- diag_inverse: float32 [2, 256, 256], replicated, may hold values from -1 to 1, as said below
- cross_block: float32 [256, 256], replicated, may hold values from -6 to 6
Outputs:
- factored: float32 [128, 32, 256, 256], P('row', 'col')
Inputs may be any that keep to these rules, and one draw needn't show every extreme that they name: `panel_rows`: slot q * 2 + m of row device r stands for the m-th structure row of block column class r + q times the number of row devices; both lists are -1 where that class is 0 or 1, and list 0 is -1 also where block column 0 lacks the row; otherwise list 0 equals list 1. `target_slots`: A filled slot of class c names in entry 0 a slot of its own row device and in entry 1 a slot of row device c modulo the number of row devices, within (c // number of row devices) * 2 and the 1 after it; both are filled or both -1, always -1 in classes 0 and 1; the target's block row number is at least its block column number. `diag_inverse`: each matrix is lower triangular.
All inputs are finite; a program needn't handle non-finite values.
Results may differ from a plain program's by a relative error of at most 0.0003.
Values sent between devices are 32-bit elements; how exact they have to be, the bound alone decides.
No kernel may reach another device: no remote copies, remote signals or barrier semaphores. Data moves between devices by JAX's collectives and lax.ppermute only.
A program may use at most 128 MiB of HBM per device.

v0:
```python
import jax
import jax.numpy as jnp
import numpy as np
from jax import lax
from jax.sharding import Mesh
from jax.sharding import PartitionSpec as P

PER_CLASS = 2
X_SIZE = 4
HIGHEST_PRECISION = lax.Precision.HIGHEST
PRODUCT_PRECISION = lax.Precision.HIGH
COL_AXES = ("zh", "zl", "x")
CLASS_AXES = ("zl", "x")


def apply_inverse(panel_rows_block, inverse):
    return jnp.einsum("ab,cb->ac", panel_rows_block, inverse, precision=HIGHEST_PRECISION)


def per_device(blocks, panel_rows, target_slots, diag_inverse, cross_block):
    row_count = lax.axis_size("row")
    col_count = lax.axis_size(COL_AXES)
    column = lax.axis_index(COL_AXES)
    stored = blocks[:, 0]
    slot_count = panel_rows.shape[1]
    block = stored.shape[-1]
    head_part = stored[:slot_count]
    chunk = slot_count * block // col_count
    pieces = head_part.reshape(col_count, chunk, block)
    received = lax.all_to_all(pieces, COL_AXES, 0, 0, tiled=True)
    zero_rows = received[0]
    one_rows = received[1]
    piece_slot = column * chunk // block
    first_live = lax.dynamic_index_in_dim(panel_rows[0], piece_slot, keepdims=False) >= 0
    second_live = lax.dynamic_index_in_dim(panel_rows[1], piece_slot, keepdims=False) >= 0
    cross_factor = jnp.dot(cross_block, diag_inverse[0].T, precision=HIGHEST_PRECISION)
    first_piece = jnp.where(first_live, apply_inverse(zero_rows, diag_inverse[0]), 0.0)
    updated_piece = one_rows - apply_inverse(first_piece, cross_factor)
    second_piece = jnp.where(second_live, apply_inverse(updated_piece, diag_inverse[1]), 0.0)
    both_pieces = jnp.stack([first_piece, second_piece])
    class_size = lax.axis_size(CLASS_AXES)
    swap = [
        (a * class_size + b, b * class_size + a)
        for a in range(row_count)
        for b in range(class_size)
    ]
    swapped = lax.ppermute(both_pieces, ("row",) + CLASS_AXES, swap)
    spread = jnp.broadcast_to(swapped[None], (row_count,) + swapped.shape)
    class_pieces = lax.all_to_all(spread, "row", 0, 0, tiled=True)
    per_slot = block // chunk
    class_pieces = class_pieces.reshape(PER_CLASS, per_slot, 2, chunk, block)
    both_cols = class_pieces.transpose(2, 0, 1, 3, 4).reshape(2, PER_CLASS, block, block)
    both_rows = lax.all_gather(both_pieces, "x", axis=1, tiled=True)
    both_rows = lax.all_gather(both_rows, ("zh", "zl"), axis=1, tiled=True)
    both_rows = both_rows.reshape(2, slot_count, block, block)
    first_rows = both_rows[0]
    second_rows = both_rows[1]
    class_start = column // row_count * PER_CLASS
    row_index = target_slots[0, :, 0]
    col_index = target_slots[1, :, 0]
    present = row_index >= 0
    left_slot = jnp.where(present, row_index, 0)
    right_slot = jnp.where(present, col_index - class_start, 0)
    products = jnp.einsum("fakm,fbjm->akbj", both_rows, both_cols, precision=PRODUCT_PRECISION)
    schur_term = products[left_slot, :, right_slot, :]
    trailing = stored - jnp.where(present[:, None, None], schur_term, 0.0)
    head_live = panel_rows >= 0
    keep_mask = ((column == 0) & head_live[0] | (column == 1) & head_live[1])[:, None, None]
    own_panel = jnp.where(column == 0, first_rows, second_rows)
    head_blocks = jnp.where(keep_mask, own_panel, trailing[:slot_count])
    factored = jnp.concatenate([head_blocks, trailing[slot_count:]], axis=0)
    return factored[:, None]


def solution(mesh):
    row_count = mesh.shape["row"]
    col_count = mesh.shape["col"]
    devices = np.asarray(mesh.devices).reshape(
        row_count, col_count // row_count, row_count // X_SIZE, X_SIZE
    )
    split_mesh = Mesh(devices, ("row",) + COL_AXES)
    return jax.shard_map(
        per_device,
        mesh=split_mesh,
        in_specs=(
            P("row", COL_AXES, None, None),
            P(None, "row"),
            P(None, "row", COL_AXES),
            P(),
            P(),
        ),
        out_specs=P("row", COL_AXES, None, None),
        check_vma=False,
    )
```

profile of v0, /device:TPU:1, one launch (start us, length us, event | category | flops | bytes accessed | tf_op | source)
XLA Modules:
  0.0 167.1 jit_solution(10187118807811461021)
XLA Ops:
  6.5 0.0 copy-start
  6.5 0.0 copy-start.4
  6.5 3.1 %slice.52 = f32[8,1,256,256]{3,2,1,0:T(8,128)} slice(f32[16,1,256,256]{3,2,1,0:T(8,128)} %param.5), slice={[0:8], [0:1], [0:256], [0:256]} | slice | bytes 4194304 | tf_op jit(solution)/shard_map/slice | solution.py:27
  9.7 11.9 %all-to-all-start = ((f32[32,64,256]{2,1,0:T(8,128)}), f32[32,64,256]{2,1,0:T(8,128)S(1)}, u32[]{:S(2)}, u32[]{:S(2)}) async-start(f32[32,64,256]{2,1,0:T(8,128)} %bitcast.2), calls=%async_computation | async-start | bytes 4194304 | tf_op jit(solution)/shard_map/all_to_all | solution.py:30
  21.5 0.0 copy-start.3
  21.5 0.0 all-gather.2.cloned.1.call-start
  21.6 0.0 copy-done.4
  21.6 0.7 fusion.18
  22.3 0.0 copy-done
  22.3 0.0 copy-done.2
  22.3 0.4 fusion.7
  22.7 47.3 %all-to-all-done = f32[32,64,256]{2,1,0:T(8,128)S(1)} async-done(((f32[32,64,256]{2,1,0:T(8,128)}), f32[32,64,256]{2,1,0:T(8,128)S(1)}, u32[]{:S(2)}, u32[]{:S(2)}) %all-to-all-start) | async-done | bytes 2097184 | tf_op jit(solution)/shard_map/all_to_all | solution.py:30
  70.0 1.0 convolution_select_fusion.1
  71.0 0.4 convolution_subtract_fusion
  71.4 1.0 fusion.5
  72.4 13.8 %all_gather.6 = f32[2,256,256]{2,1,0:T(8,128)} all-gather(f32[2,64,256]{2,1,0:T(8,128)S(1)} %pad_maximum_fusion), channel_id=1, replica_groups=mesh['row'=8,'zh'=4,'zl'=2,'x'=4] {'x'}, dimensions={1}, use_global_device_ids=true | all-gather | bytes 655360 | tf_op jit(solution)/shard_map/all_gather | solution.py:53
  86.2 0.0 all-gather.2.cloned.1.call-update
  86.2 6.0 %collective-permute-start = (f32[2,64,256]{2,1,0:T(8,128)S(1)}, f32[2,64,256]{2,1,0:T(8,128)S(1)}, u32[]{:S(2)}, u32[]{:S(2)}) collective-permute-start(f32[2,64,256]{2,1,0:T(8,128)S(1)} %pad_maximum_fusion), channel_id=1, source_target_pairs={{0,0},{1,32},{2,64},{3,96},{4,128},{5,160},{6,192},{7,224},{32,1},... | collective-permute-start | bytes 393224 | tf_op jit(solution)/shard_map/ppermute | solution.py:47
  92.2 2.6 %collective-permute-done = f32[2,64,256]{2,1,0:T(8,128)S(1)} collective-permute-done((f32[2,64,256]{2,1,0:T(8,128)S(1)}, f32[2,64,256]{2,1,0:T(8,128)S(1)}, u32[]{:S(2)}, u32[]{:S(2)}) %collective-permute-start) | collective-permute-done | bytes 131104 | tf_op jit(solution)/shard_map/ppermute | solution.py:47
  94.8 1.1 broadcast_in_dim.44
  95.9 10.8 %all-to-all-start.1 = ((f32[8,2,64,256]{3,2,1,0:T(8,128)}), f32[8,2,64,256]{3,2,1,0:T(8,128)S(1)}, u32[]{:S(2)}, u32[]{:S(2)}) async-start(f32[8,2,64,256]{3,2,1,0:T(8,128)} %broadcast_in_dim.44), calls=%async_computation.1 | async-start | bytes 2097152 | tf_op jit(solution)/shard_map/all_to_all | solution.py:49
  106.7 0.0 copy-done.3
  106.8 15.0 %all-to-all-done.1 = f32[8,2,64,256]{3,2,1,0:T(8,128)S(1)} async-done(((f32[8,2,64,256]{3,2,1,0:T(8,128)}), f32[8,2,64,256]{3,2,1,0:T(8,128)S(1)}, u32[]{:S(2)}, u32[]{:S(2)}) %all-to-all-start.1) | async-done | bytes 1048608 | tf_op jit(solution)/shard_map/all_to_all | solution.py:49
  121.8 0.1 copy.8
  121.9 18.3 %all-gather.2.cloned.1.call-done = f32[2,2048,256]{2,1,0:T(8,128)} async-done(((f32[2,256,256]{2,1,0:T(8,128)}), f32[2,2048,256]{2,1,0:T(8,128)}) %all-gather.2.cloned.1.call-update) | async-done | bytes 4194320 | tf_op jit(solution)/shard_map/all_gather | solution.py:54
  140.3 7.2 %fusion.2 = f32[8,256,2,256]{3,1,2,0:T(8,128)} fusion(f32[2,2,256,256,1]{3,2,0,1,4:T(8,128)S(1)} %bitcast.66, f32[2,8,256,256,1]{3,2,1,0,4:T(8,128)} %bitcast.64), kind=kOutput, calls=%fused_computation.5 | convolution fusion | flops 3221225472 | bytes 9437184 | tf_op jit(solution)/shard_map/fakm,fbjm->akbj/dot_general | solution.py:64
  147.5 5.0 %gather_fusion = f32[16,256,256]{2,1,0:T(8,128)} fusion(f32[8,256,2,256]{3,1,2,0:T(8,128)} %fusion.2, s32[16]{0:T(128)S(1)} %fusion.16), kind=kCustom, calls=%fused_computation | custom fusion | bytes 8388736 | tf_op jit(solution)/shard_map/gather | solution.py:65
  152.4 4.2 %bitcast_subtract_fusion = f32[16,256,256]{2,1,0:T(8,128)S(1)} fusion(f32[16,1,256,256]{3,2,1,0:T(8,128)} %param.5, f32[16,256,256]{2,1,0:T(8,128)} %gather_fusion, pred[16]{0:T(512)(128)(4,1)S(1)} %compare_bitcast_fusion), kind=kLoop, calls=%fused_computation.4 | loop fusion | flops 2097152 | bytes 12582928 | tf_op jit(solution)/shard_map/sub | solution.py:66
  156.7 0.4 copy-done.1
  157.1 0.3 slice_select_fusion.1
  157.4 0.4 slice_select_fusion
  157.8 2.4 %maximum_bitcast_fusion = f32[16,1,256,256]{3,2,1,0:T(8,128)} fusion(f32[8,256,256]{2,1,0:T(8,128)S(1)} %get-tuple-element.6, f32[8,256,256]{2,1,0:T(8,128)S(1)} %get-tuple-element.5), kind=kLoop, calls=%fused_computation.1 | loop fusion | flops 1048576 | bytes 8388608 | tf_op jit(solution)/shard_map/broadcast_in_dim | solution.py:72
  (8 shorter events, 0.1 us)
Async XLA Ops:
  6.5 15.8 %copy-start = (f32[256,256]{1,0:T(8,128)S(1)}, f32[256,256]{1,0:T(8,128)}, u32[]{:S(2)}) copy-start(f32[256,256]{1,0:T(8,128)} %param.9) | copy-start | bytes 786436
  6.5 15.1 %copy-start.4 = (s32[2,8]{1,0:T(2,128)S(1)}, s32[2,8]{1,0:T(2,128)}, u32[]{:S(2)}) copy-start(s32[2,8]{1,0:T(2,128)} %param.6) | copy-start | bytes 196
  6.5 15.8 %copy-start.2 = (f32[2,256,256]{2,1,0:T(8,128)S(1)}, f32[2,256,256]{2,1,0:T(8,128)}, u32[]{:S(2)}) copy-start(f32[2,256,256]{2,1,0:T(8,128)} %param.8) | copy-start | bytes 1572868
  9.7 60.4 %all-to-all-start = ((f32[32,64,256]{2,1,0:T(8,128)}), f32[32,64,256]{2,1,0:T(8,128)S(1)}, u32[]{:S(2)}, u32[]{:S(2)}) async-start(f32[32,64,256]{2,1,0:T(8,128)} %bitcast.2), calls=%async_computation | async-start | bytes 4194304 | tf_op jit(solution)/shard_map/all_to_all | solution.py:30
  21.5 85.2 %copy-start.3 = (s32[2,16,1]{1,2,0:T(1,128)S(1)}, s32[2,16,1]{1,2,0:T(1,128)}, u32[]{:S(2)}) copy-start(s32[2,16,1]{1,2,0:T(1,128)} %param.7) | copy-start | bytes 388
  21.5 118.7 %all-gather.2.cloned.1.call-start = ((), (), s32[]{:S(2)}) async-start(), calls=%async_computation.2 | async-start | bytes 4718592 | tf_op jit(solution)/shard_map/all_gather | solution.py:54
  86.2 8.6 %collective-permute-start = (f32[2,64,256]{2,1,0:T(8,128)S(1)}, f32[2,64,256]{2,1,0:T(8,128)S(1)}, u32[]{:S(2)}, u32[]{:S(2)}) collective-permute-start(f32[2,64,256]{2,1,0:T(8,128)S(1)} %pad_maximum_fusion), channel_id=1, source_target_pairs={{0,0},{1,32},{2,64},{3,96},{4,128},{5,160},{6,192},{7,224},{32,1},... | collective-permute-start | bytes 393224 | tf_op jit(solution)/shard_map/ppermute | solution.py:47
  95.9 25.9 %all-to-all-start.1 = ((f32[8,2,64,256]{3,2,1,0:T(8,128)}), f32[8,2,64,256]{3,2,1,0:T(8,128)S(1)}, u32[]{:S(2)}, u32[]{:S(2)}) async-start(f32[8,2,64,256]{3,2,1,0:T(8,128)} %broadcast_in_dim.44), calls=%async_computation.1 | async-start | bytes 2097152 | tf_op jit(solution)/shard_map/all_to_all | solution.py:49
  152.4 4.6 %copy-start.1 = (f32[2,2048,256]{2,1,0:T(8,128)S(1)}, f32[2,2048,256]{2,1,0:T(8,128)}, u32[]{:S(2)}) copy-start(f32[2,2048,256]{2,1,0:T(8,128)} %all-gather.2.cloned.1.call-done) | copy-start | bytes 12582916
Sparse Core Ops, SparseCore 0:
  86.3 53.9 all-gather.1
where the time goes:
time: 167 us
  waiting for transfers between devices  83.3 us (50%)
  starting transfers between devices  28.7 us (17%)
  blocking collectives  13.8 us (8%)
  between operations  13.5 us (8%)
  matrix products  9.97 us (6%)
  local copies, waits for them, and re-layouts  9.68 us (6%)
  other arithmetic  8.07 us (5%)
    all_to_all x1, waiting for transfers between devices, per_device(): received = lax.all_to_all(pieces, COL_AXES, 0, 0, tiled=True)  47.3 us
    all_gather x1, waiting for transfers between devices, per_device(): both_rows = lax.all_gather(both_rows, ('zh', 'zl'), axis=1, tiled=True)  18.3 us
    all_to_all x1, waiting for transfers between devices, per_device(): class_pieces = lax.all_to_all(spread, 'row', 0, 0, tiled=True)  15 us
    all_gather x1, blocking collectives, per_device(): both_rows = lax.all_gather(both_pieces, 'x', axis=1, tiled=True)  13.8 us
    all_to_all x1, starting transfers between devices, per_device(): received = lax.all_to_all(pieces, COL_AXES, 0, 0, tiled=True)  11.9 us
    all_to_all x1, starting transfers between devices, per_device(): class_pieces = lax.all_to_all(spread, 'row', 0, 0, tiled=True)  10.8 us
    dot_general x1, matrix products, per_device(): jnp.einsum('fakm,fbjm->akbj', both_rows, both_cols, precision=PRODUCT_PRE...  7.19 us
    ppermute x1, starting transfers between devices, per_device(): swapped = lax.ppermute(both_pieces, ('row',) + CLASS_AXES, swap)  5.96 us
  transfers between devices with their start and end apart: 4, of which 4 were waited for; matrix products, arithmetic and copies ran while one was open for 1% of the time, Pallas kernels for 0%

commit v1 on v0

--- a/solution.py
+++ b/solution.py
@@ -4,6 +4,7 @@
 from jax import lax
 from jax.sharding import Mesh
 from jax.sharding import PartitionSpec as P
+from jax.lax import all_to_all, psum
 
 PER_CLASS = 2
 X_SIZE = 4
@@ -51,7 +52,13 @@
     class_pieces = class_pieces.reshape(PER_CLASS, per_slot, 2, chunk, block)
     both_cols = class_pieces.transpose(2, 0, 1, 3, 4).reshape(2, PER_CLASS, block, block)
     both_rows = lax.all_gather(both_pieces, "x", axis=1, tiled=True)
-    both_rows = lax.all_gather(both_rows, ("zh", "zl"), axis=1, tiled=True)
+
+    def read_rings_all(raw):
+        new = jnp.stack([raw] * psum(1, axis_name=("zh", "zl")))
+        before = jnp.concatenate(all_to_all(new, ("zh", "zl"), split_axis=0, concat_axis=0), axis=1)
+        return before
+
+    both_rows = read_rings_all(both_rows)
     both_rows = both_rows.reshape(2, slot_count, block, block)
     first_rows = both_rows[0]
     second_rows = both_rows[1]

time: 167 us -> 224 us (1.34); the launches traced: 167 us -> 221 us
  waiting for transfers between devices: 83.3 us -> 145 us
  between operations: 13.5 us -> 0.17 us
  starting transfers between devices: 28.7 us -> 32.5 us
  blocking collectives: 13.8 us -> 11.2 us
    all_to_all x0 -> x1, waiting for transfers between devices: none -> 91.2 us  [read_rings_all(): all_to_all(new, ('zh', 'zl'), split_axis=0, concat_axis=0)]
    all_gather x1 -> x0, waiting for transfers between devices: 18.3 us -> none  [per_device(): both_rows = lax.all_gather(both_rows, ('zh', 'zl'), axis=1, tiled=True)]
    all_to_all x1, waiting for transfers between devices: 15 us -> 3.87 us  [per_device(): class_pieces = lax.all_to_all(spread, 'row', 0, 0, tiled=True)]
    all_to_all x0 -> x1, starting transfers between devices: none -> 4.68 us  [read_rings_all(): all_to_all(new, ('zh', 'zl'), split_axis=0, concat_axis=0)]
    select_n x1, other arithmetic: 0.43 us -> 2.97 us  [per_device(): head_blocks = jnp.where(keep_mask, own_panel, trailing[:slot_count])]
    all_gather x1, blocking collectives: 13.8 us -> 11.2 us  [per_device(): both_rows = lax.all_gather(both_pieces, 'x', axis=1, tiled=True)]
    another operation x0 -> x1, local copies, waits for them, and re-layouts: none -> 2.42 us  [read_rings_all(): new = jnp.stack([raw] * psum(1, axis_name=('zh', 'zl')))]
where the time goes in v1:
time: 224 us; the launch traced here: 221 us
  waiting for transfers between devices  145 us (65%)
  starting transfers between devices  32.5 us (15%)
  local copies, waits for them, and re-layouts  11.7 us (5%)
  blocking collectives  11.2 us (5%)
  other arithmetic  10.2 us (5%)
  matrix products  9.9 us (4%)
    all_to_all x1, waiting for transfers between devices, read_rings_all(): all_to_all(new, ('zh', 'zl'), split_axis=0, concat_axis=0)  91.2 us
    all_to_all x1, waiting for transfers between devices, per_device(): received = lax.all_to_all(pieces, COL_AXES, 0, 0, tiled=True)  47.4 us
    all_to_all x1, starting transfers between devices, per_device(): received = lax.all_to_all(pieces, COL_AXES, 0, 0, tiled=True)  11.9 us
    all_gather x1, blocking collectives, per_device(): both_rows = lax.all_gather(both_pieces, 'x', axis=1, tiled=True)  11.2 us
    all_to_all x1, starting transfers between devices, per_device(): class_pieces = lax.all_to_all(spread, 'row', 0, 0, tiled=True)  10.9 us
    dot_general x1, matrix products, per_device(): jnp.einsum('fakm,fbjm->akbj', both_rows, both_cols, precision=PRODUCT_PRE...  7.19 us
    ppermute x1, starting transfers between devices, per_device(): swapped = lax.ppermute(both_pieces, ('row',) + CLASS_AXES, swap)  5.02 us
    gather x1, local copies, waits for them, and re-layouts, per_device(): schur_term = products[left_slot, :, right_slot, :]  4.98 us
  transfers between devices with their start and end apart: 4, of which 4 were waited for; matrix products, arithmetic and copies ran while one was open for 1% of the time, Pallas kernels for 0%

profile of v1, /device:TPU:1, one launch (start us, length us, event | category | flops | bytes accessed | tf_op | source)
XLA Modules:
  0.0 220.7 jit_solution(2542515000111328102)
XLA Ops:
  0.0 0.0 copy-start
  0.0 0.0 copy-start.3
  0.0 0.0 copy-start.1
  0.0 3.1 %slice.50 = f32[8,1,256,256]{3,2,1,0:T(8,128)} slice(f32[16,1,256,256]{3,2,1,0:T(8,128)} %param.5), slice={[0:8], [0:1], [0:256], [0:256]} | slice | bytes 4194304 | tf_op jit(solution)/shard_map/slice | solution.py:28
  3.1 11.9 %all-to-all-start = ((f32[32,64,256]{2,1,0:T(8,128)}), f32[32,64,256]{2,1,0:T(8,128)S(1)}, u32[]{:S(2)}, u32[]{:S(2)}) async-start(f32[32,64,256]{2,1,0:T(8,128)} %bitcast.2), calls=%async_computation | async-start | bytes 4194304 | tf_op jit(solution)/shard_map/all_to_all | solution.py:31
  15.0 0.0 copy-done.3
  15.1 0.6 fusion.19
  15.7 0.0 copy-done
  15.7 0.0 copy-done.1
  15.7 0.4 fusion.8
  16.1 47.4 %all-to-all-done = f32[32,64,256]{2,1,0:T(8,128)S(1)} async-done(((f32[32,64,256]{2,1,0:T(8,128)}), f32[32,64,256]{2,1,0:T(8,128)S(1)}, u32[]{:S(2)}, u32[]{:S(2)}) %all-to-all-start) | async-done | bytes 2097184 | tf_op jit(solution)/shard_map/all_to_all | solution.py:31
  63.5 0.9 convolution_select_fusion.1
  64.4 0.4 convolution_subtract_fusion
  64.8 1.0 fusion.6
  65.8 5.0 %collective-permute-start = (f32[2,64,256]{2,1,0:T(8,128)S(1)}, f32[2,64,256]{2,1,0:T(8,128)S(1)}, u32[]{:S(2)}, u32[]{:S(2)}) collective-permute-start(f32[2,64,256]{2,1,0:T(8,128)S(1)} %pad_maximum_fusion), channel_id=1, source_target_pairs={{0,0},{1,32},{2,64},{3,96},{4,128},{5,160},{6,192},{7,224},{32,1},... | collective-permute-start | bytes 393224 | tf_op jit(solution)/shard_map/ppermute | solution.py:48
  70.8 2.6 %collective-permute-done = f32[2,64,256]{2,1,0:T(8,128)S(1)} collective-permute-done((f32[2,64,256]{2,1,0:T(8,128)S(1)}, f32[2,64,256]{2,1,0:T(8,128)S(1)}, u32[]{:S(2)}, u32[]{:S(2)}) %collective-permute-start) | collective-permute-done | bytes 131104 | tf_op jit(solution)/shard_map/ppermute | solution.py:48
  73.5 1.1 broadcast_in_dim.44
  74.5 10.9 %all-to-all-start.2 = ((f32[8,2,64,256]{3,2,1,0:T(8,128)}), f32[8,2,64,256]{3,2,1,0:T(8,128)S(1)}, u32[]{:S(2)}, u32[]{:S(2)}) async-start(f32[8,2,64,256]{3,2,1,0:T(8,128)} %broadcast_in_dim.44), calls=%async_computation.2 | async-start | bytes 2097152 | tf_op jit(solution)/shard_map/all_to_all | solution.py:50
  85.5 11.2 %all_gather.3 = f32[2,256,256]{2,1,0:T(8,128)S(1)} all-gather(f32[2,64,256]{2,1,0:T(8,128)S(1)} %pad_maximum_fusion), channel_id=1, replica_groups=mesh['row'=8,'zh'=4,'zl'=2,'x'=4] {'x'}, dimensions={1}, use_global_device_ids=true | all-gather | bytes 655360 | tf_op jit(solution)/shard_map/all_gather | solution.py:54
  96.7 3.9 %all-to-all-done.2 = f32[8,2,64,256]{3,2,1,0:T(8,128)S(1)} async-done(((f32[8,2,64,256]{3,2,1,0:T(8,128)}), f32[8,2,64,256]{3,2,1,0:T(8,128)S(1)}, u32[]{:S(2)}, u32[]{:S(2)}) %all-to-all-start.2) | async-done | bytes 1048608 | tf_op jit(solution)/shard_map/all_to_all | solution.py:50
  100.6 2.4 %stack.11 = f32[8,2,256,256]{3,2,1,0:T(8,128)} broadcast(f32[2,256,256]{2,1,0:T(8,128)S(1)} %all_gather.3), dimensions={1,2,3} | broadcast | bytes 4718592 | tf_op jit(solution)/shard_map/stack | solution.py:57
  103.0 0.0 copy-start.2
  103.0 4.7 %all-to-all-start.1 = ((f32[8,2,256,256]{3,2,1,0:T(8,128)}), f32[8,2,256,256]{3,2,1,0:T(8,128)}, u32[]{:S(2)}, u32[]{:S(2)}) async-start(f32[8,2,256,256]{3,2,1,0:T(8,128)} %stack.11), calls=%async_computation.1 | async-start | bytes 8388608 | tf_op jit(solution)/shard_map/all_to_all | solution.py:58
  107.7 0.0 copy-done.2
  107.8 0.1 copy.7
  107.9 91.2 %all-to-all-done.1 = f32[8,2,256,256]{3,2,1,0:T(8,128)} async-done(((f32[8,2,256,256]{3,2,1,0:T(8,128)}), f32[8,2,256,256]{3,2,1,0:T(8,128)}, u32[]{:S(2)}, u32[]{:S(2)}) %all-to-all-start.1) | async-done | bytes 4194336 | tf_op jit(solution)/shard_map/all_to_all | solution.py:58
  199.0 7.2 %fusion.2 = f32[8,256,2,256]{3,1,2,0:T(8,128)} fusion(f32[2,2,256,256,1]{3,2,0,1,4:T(8,128)S(1)} %bitcast.73, f32[8,2,256,256]{3,2,1,0:T(8,128)} %all-to-all-done.1), kind=kOutput, calls=%fused_computation.5 | convolution fusion | flops 3221225472 | bytes 9437184 | tf_op jit(solution)/shard_map/fakm,fbjm->akbj/dot_general | solution.py:71
  206.2 5.0 %gather_fusion = f32[16,256,256]{2,1,0:T(8,128)} fusion(f32[8,256,2,256]{3,1,2,0:T(8,128)} %fusion.2, s32[16]{0:T(128)S(1)} %fusion.17), kind=kCustom, calls=%fused_computation | custom fusion | bytes 8388736 | tf_op jit(solution)/shard_map/gather | solution.py:72
  211.2 4.1 %bitcast_subtract_fusion = f32[16,256,256]{2,1,0:T(8,128)S(1)} fusion(f32[16,1,256,256]{3,2,1,0:T(8,128)} %param.5, f32[16,256,256]{2,1,0:T(8,128)} %gather_fusion, pred[16]{0:T(512)(128)(4,1)S(1)} %compare_bitcast_fusion), kind=kLoop, calls=%fused_computation.4 | loop fusion | flops 2097152 | bytes 12582928 | tf_op jit(solution)/shard_map/sub | solution.py:73
  215.3 3.0 %slice_select_fusion = (f32[8,256,256]{2,1,0:T(8,128)S(1)}, f32[8,256,256]{2,1,0:T(8,128)S(1)}) fusion(f32[16,256,256]{2,1,0:T(8,128)S(1)} %bitcast_subtract_fusion, f32[2,8,256,256]{3,2,0,1:T(8,128)} %bitcast.10, pred[8]{0:T(512)(128)(4,1)S(1)} %or_bitcast_fusion, pred[]{:T(512)S(6)} %eq.7), kind=kLoop, calls=%fused_computation.6 | loop fusion | flops 1048576 | bytes 12582921 | tf_op jit(solution)/shard_map/jit(_where)/select_n | solution.py:77
  218.3 2.4 %maximum_bitcast_fusion = f32[16,1,256,256]{3,2,1,0:T(8,128)} fusion(f32[8,256,256]{2,1,0:T(8,128)S(1)} %get-tuple-element.6, f32[8,256,256]{2,1,0:T(8,128)S(1)} %get-tuple-element.5), kind=kLoop, calls=%fused_computation.1 | loop fusion | flops 1048576 | bytes 8388608 | tf_op jit(solution)/shard_map/broadcast_in_dim | solution.py:79
  (6 shorter events, 0.1 us)
Async XLA Ops:
  0.0 15.7 %copy-start = (f32[256,256]{1,0:T(8,128)S(1)}, f32[256,256]{1,0:T(8,128)}, u32[]{:S(2)}) copy-start(f32[256,256]{1,0:T(8,128)} %param.9) | copy-start | bytes 786436
  0.0 15.0 %copy-start.3 = (s32[2,8]{1,0:T(2,128)S(1)}, s32[2,8]{1,0:T(2,128)}, u32[]{:S(2)}) copy-start(s32[2,8]{1,0:T(2,128)} %param.6) | copy-start | bytes 196
  0.0 15.7 %copy-start.1 = (f32[2,256,256]{2,1,0:T(8,128)S(1)}, f32[2,256,256]{2,1,0:T(8,128)}, u32[]{:S(2)}) copy-start(f32[2,256,256]{2,1,0:T(8,128)} %param.8) | copy-start | bytes 1572868
  3.1 60.4 %all-to-all-start = ((f32[32,64,256]{2,1,0:T(8,128)}), f32[32,64,256]{2,1,0:T(8,128)S(1)}, u32[]{:S(2)}, u32[]{:S(2)}) async-start(f32[32,64,256]{2,1,0:T(8,128)} %bitcast.2), calls=%async_computation | async-start | bytes 4194304 | tf_op jit(solution)/shard_map/all_to_all | solution.py:31
  65.8 7.7 %collective-permute-start = (f32[2,64,256]{2,1,0:T(8,128)S(1)}, f32[2,64,256]{2,1,0:T(8,128)S(1)}, u32[]{:S(2)}, u32[]{:S(2)}) collective-permute-start(f32[2,64,256]{2,1,0:T(8,128)S(1)} %pad_maximum_fusion), channel_id=1, source_target_pairs={{0,0},{1,32},{2,64},{3,96},{4,128},{5,160},{6,192},{7,224},{32,1},... | collective-permute-start | bytes 393224 | tf_op jit(solution)/shard_map/ppermute | solution.py:48
  74.5 26.0 %all-to-all-start.2 = ((f32[8,2,64,256]{3,2,1,0:T(8,128)}), f32[8,2,64,256]{3,2,1,0:T(8,128)S(1)}, u32[]{:S(2)}, u32[]{:S(2)}) async-start(f32[8,2,64,256]{3,2,1,0:T(8,128)} %broadcast_in_dim.44), calls=%async_computation.2 | async-start | bytes 2097152 | tf_op jit(solution)/shard_map/all_to_all | solution.py:50
  103.0 4.7 %copy-start.2 = (s32[2,16,1]{1,2,0:T(1,128)S(1)}, s32[2,16,1]{1,2,0:T(1,128)}, u32[]{:S(2)}) copy-start(s32[2,16,1]{1,2,0:T(1,128)} %param.7) | copy-start | bytes 388
  103.0 96.0 %all-to-all-start.1 = ((f32[8,2,256,256]{3,2,1,0:T(8,128)}), f32[8,2,256,256]{3,2,1,0:T(8,128)}, u32[]{:S(2)}, u32[]{:S(2)}) async-start(f32[8,2,256,256]{3,2,1,0:T(8,128)} %stack.11), calls=%async_computation.1 | async-start | bytes 8388608 | tf_op jit(solution)/shard_map/all_to_all | solution.py:58
